TPU v7x, 128 devices: a whole 4x4x4 slice. The times are simulated.
128 devices in a mesh: grp: 8 (over z, core), dev: 16 (over y, x).
Axes of the slice: x: 4, y: 4, z: 4, core: 2. Of those that a mesh axis runs over, the one named last changes fastest.
Arguments:
- positions: float32 [3, 131072], P(None, ('grp', 'dev')), may hold values from -3 to 3
- velocities: float32 [3, 131072], P(None, ('grp', 'dev')), may hold values from -5 to 5
- accelerations: float32 [3, 131072], P(None, ('grp', 'dev')), may hold values from -3 to 3
- jerks: float32 [3, 131072], P(None, ('grp', 'dev')), may hold values from -3 to 3
- levels: int32 [131072], P(('grp', 'dev')), may hold values from 0 to 5
- counts: int32 [2, 128], replicated, may hold values from 1 to 256, 16384 in all within a row
- active_rows: int32 [2, 32768], P(None, ('grp', 'dev')), may hold values from 0 to 1023, as said below
Outputs:
- new_positions: float32 [3, 131072], P(None, ('grp', 'dev'))
- new_velocities: float32 [3, 131072], P(None, ('grp', 'dev'))
- new_accelerations: float32 [3, 131072], P(None, ('grp', 'dev'))
- new_jerks: float32 [3, 131072], P(None, ('grp', 'dev'))
Inputs may be any that keep to these rules, and one draw needn't show every extreme that they name: In each step the 128 counts sum to exactly 16384 and the largest of them is exactly 256. `active_rows`: for each step and device, the 256 entries of the device's slots are distinct indices of that device's own stars; only the first counts of them are live.
All inputs are finite; a program needn't handle non-finite values.
Results may differ from a plain program's by a relative error of at most 0.00022.
Values sent between devices are 32-bit elements; how exact they have to be, the bound alone decides.
No kernel may reach another device: no remote copies, remote signals or barrier semaphores. Data moves between devices by JAX's collectives and lax.ppermute only.
A program may use at most 128 MiB of HBM per device.

v0:
```python
import math
import jax
import jax.numpy as jnp
from jax import lax
from jax.sharding import PartitionSpec as P

tick_length = 1.0 / 128.0


def pair_block(targets, src_pos, src_vel, mass, soft_sq):
    gap_x = src_pos[0][None, :] - targets[0][:, None]
    gap_y = src_pos[1][None, :] - targets[1][:, None]
    gap_z = src_pos[2][None, :] - targets[2][:, None]
    drift_x = src_vel[0][None, :] - targets[3][:, None]
    drift_y = src_vel[1][None, :] - targets[4][:, None]
    drift_z = src_vel[2][None, :] - targets[5][:, None]
    squared = gap_x * gap_x + gap_y * gap_y + gap_z * gap_z + soft_sq
    inverse = lax.rsqrt(squared)
    weight = mass * inverse * inverse * inverse
    along = 3.0 * (gap_x * drift_x + gap_y * drift_y + gap_z * drift_z) * inverse * inverse
    return jnp.stack(
        [
            jnp.sum(weight * gap_x, axis=1),
            jnp.sum(weight * gap_y, axis=1),
            jnp.sum(weight * gap_z, axis=1),
            jnp.sum(weight * (drift_x - along * gap_x), axis=1),
            jnp.sum(weight * (drift_y - along * gap_y), axis=1),
            jnp.sum(weight * (drift_z - along * gap_z), axis=1),
        ]
    )


def block_terms(packed, src_pos, src_vel, mass, soft_sq):
    width, total = packed.shape
    block = math.gcd(total, 2048)
    grouped = packed.reshape(width, total // block, block).transpose(1, 0, 2)
    result = lax.map(lambda targets: pair_block(targets, src_pos, src_vel, mass, soft_sq), grouped)
    return result.transpose(1, 0, 2).reshape(width, total)


def predict(positions, velocities, accelerations, jerks, elapsed):
    span = elapsed[None, :]
    pred_pos = (
        positions
        + span * velocities
        + 0.5 * span * span * accelerations
        + span * span * span / 6.0 * jerks
    )
    pred_vel = velocities + span * accelerations + 0.5 * span * span * jerks
    return (pred_pos, pred_vel)


def correct(old_pos, old_vel, old_acc, old_jerk, force, jerk_new, span):
    span = span[None, :]
    new_vel = old_vel + 0.5 * span * (old_acc + force) + span * span / 12.0 * (old_jerk - jerk_new)
    new_pos = old_pos + 0.5 * span * (old_vel + new_vel) + span * span / 12.0 * (old_acc - force)
    return (new_pos, new_vel)


def shards(positions, velocities, accelerations, jerks, levels, counts, active_rows):
    devices_all = lax.axis_size("grp") * lax.axis_size("dev")
    my_rank = lax.axis_index("grp") * lax.axis_size("dev") + lax.axis_index("dev")
    star_dev = positions.shape[1]
    slot_cap = active_rows.shape[1]
    stars_all = star_dev * devices_all
    live_all = stars_all // 8
    mass = 1.0 / stars_all
    soft_sq = 0.0004 * (131072.0 / stars_all) ** (2.0 / 3.0)
    chunks = 4
    chunk = live_all // chunks
    last_time = -(jnp.left_shift(jnp.int32(1), levels) - 1).astype(jnp.float32) * tick_length
    for step in range(active_rows.shape[0]):
        now = (step + 1) * tick_length
        pred_pos, pred_vel = predict(positions, velocities, accelerations, jerks, now - last_time)
        rows = active_rows[step]
        targets = jnp.concatenate([pred_pos[:, rows], pred_vel[:, rows]], axis=0)
        step_counts = counts[step]
        own_count = step_counts[my_rank]
        inclusive = jnp.cumsum(step_counts).astype(jnp.int32)
        first = inclusive - step_counts
        place = jnp.arange(live_all, dtype=jnp.int32)
        owner = jnp.sum((inclusive[None, :] <= place[:, None]).astype(jnp.int32), axis=1)
        owner = jnp.minimum(owner, devices_all - 1)
        slot = owner * slot_cap + place - first[owner]
        gathered = lax.all_gather(targets[None], ("grp", "dev"), axis=0, tiled=True)
        flat = gathered.transpose(1, 0, 2).reshape(6, devices_all * slot_cap)
        compact = flat[:, slot]
        parts = []
        summed = None
        for c in range(chunks):
            piece = compact[:, c * chunk : (c + 1) * chunk]
            terms = block_terms(piece, pred_pos, pred_vel, mass, soft_sq)
            if summed is not None:
                terms, summed = lax.optimization_barrier((terms, summed))
                parts.append(summed)
            summed = lax.psum(terms, ("grp", "dev"))
        parts.append(summed)
        parts.append(jnp.zeros((6, slot_cap), jnp.float32))
        totals = jnp.concatenate(parts, axis=1)
        own = lax.dynamic_slice_in_dim(totals, first[my_rank], slot_cap, 1)
        span = now - last_time[rows]
        new_pos, new_vel = correct(
            positions[:, rows],
            velocities[:, rows],
            accelerations[:, rows],
            jerks[:, rows],
            own[:3],
            own[3:],
            span,
        )
        live = jnp.arange(slot_cap, dtype=jnp.int32) < own_count
        target = jnp.where(live, rows, star_dev)
        positions = positions.at[:, target].set(new_pos, mode="drop")
        velocities = velocities.at[:, target].set(new_vel, mode="drop")
        accelerations = accelerations.at[:, target].set(own[:3], mode="drop")
        jerks = jerks.at[:, target].set(own[3:], mode="drop")
        last_time = last_time.at[target].set(now, mode="drop")
    return (positions, velocities, accelerations, jerks)


def solution(mesh):
    placed = (
        P(None, ("grp", "dev")),
        P(None, ("grp", "dev")),
        P(None, ("grp", "dev")),
        P(None, ("grp", "dev")),
        P(("grp", "dev")),
        P(),
        P(None, ("grp", "dev")),
    )
    return jax.shard_map(
        shards,
        mesh=mesh,
        in_specs=placed,
        out_specs=(
            P(None, ("grp", "dev")),
            P(None, ("grp", "dev")),
            P(None, ("grp", "dev")),
            P(None, ("grp", "dev")),
        ),
        check_vma=False,
    )
```

profile of v0, /device:TPU:1, one launch (start us, length us, event | category | flops | bytes accessed | tf_op | source)
XLA Modules:
  0.0 1731.8 jit_solution(9103468403013295511)
XLA Ops:
  8.6 2.6 compare_select_fusion.4
  14.8 63.9 %all-gather.2 = f32[128,6,256]{2,1,0:T(8,128)S(1)} all-gather(f32[1,6,256]{2,1,0:T(8,128)S(1)} %maximum_bitcast_fusion), channel_id=2, replica_groups=mesh['grp'=8,'dev'=16] {'grp','dev'}, dimensions={0}, use_global_device_ids=true | all-gather | bytes 792576 | tf_op jit(solution)/shard_map/all_gather | solution.py:85
  78.7 8.4 copy.253
  87.8 2.3 convert_reduce_fusion.1
  90.3 97.2 %gather_fusion.6 = s32[16384]{0:T(1024)S(1)} fusion(s32[128]{0:T(128)S(1)} %get-tuple-element.734, s32[16384]{0:T(1024)S(1)} %broadcast_clamp_fusion.3), kind=kCustom, calls=%fused_computation.6 | custom fusion | bytes 196608 | tf_op jit(solution)/shard_map/gather | solution.py:84
  187.7 60.2 %gather_fusion.7 = f32[16384,6]{1,0:T(8,128)} fusion(f32[6,32768]{0,1:T(8,128)} %bitcast.632, s32[16384]{0:T(1024)S(1)} %broadcast_clamp_fusion.1), kind=kCustom, calls=%fused_computation.7 | custom fusion | bytes 851968 | tf_op jit(solution)/shard_map/gather | solution.py:87
  247.9 6.2 fusion.167
  254.0 2.2 copy.256
  256.3 32.8 %while.81 = (s32[]{:T(128)}, f32[2,6,2048]{2,1,0:T(8,128)S(1)}, f32[3,1024]{1,0:T(4,128)S(1)}, f32[2,6,2048]{2,1,0:T(8,128)S(1)}, f32[3,1024]{1,0:T(4,128)S(1)},...) while((s32[]{:T(128)}, f32[2,6,2048]{2,1,0:T(8,128)S(1)}, ...), condition=%wide.region_17.18_spmd, body=%wide.region_10.17_spmd.sunk | while | flops 85970952 | bytes 499925 | solution.py:37
  256.4 16.2 fusion.187
  272.8 16.2 fusion.187
  290.1 2.3 convert_reduce_fusion
  292.5 2.2 copy.255
  294.7 32.8 %while.80 = (s32[]{:T(128)}, f32[2,6,2048]{2,1,0:T(8,128)S(1)}, f32[3,1024]{1,0:T(4,128)S(1)}, f32[2,6,2048]{2,1,0:T(8,128)S(1)}, f32[3,1024]{1,0:T(4,128)S(1)},...) while((s32[]{:T(128)}, f32[2,6,2048]{2,1,0:T(8,128)S(1)}, ...), condition=%wide.region_9.10_spmd, body=%wide.region_2.9_spmd.sunk | while | flops 85970952 | bytes 499925 | solution.py:37
  294.8 16.2 fusion.185
  311.2 16.2 fusion.185
  327.5 2.3 copy.257
  329.8 32.8 %while.82 = (s32[]{:T(128)}, f32[2,6,2048]{2,1,0:T(8,128)S(1)}, f32[3,1024]{1,0:T(4,128)S(1)}, f32[2,6,2048]{2,1,0:T(8,128)S(1)}, f32[3,1024]{1,0:T(4,128)S(1)},...) while((s32[]{:T(128)}, f32[2,6,2048]{2,1,0:T(8,128)S(1)}, ...), condition=%wide.region_26.27_spmd, body=%wide.region_19.26_spmd.sunk | while | flops 85970952 | bytes 499925 | solution.py:37
  329.9 16.2 fusion.189
  346.4 16.2 fusion.189
  363.3 32.9 %while.83 = (s32[]{:T(128)}, f32[2,6,2048]{2,1,0:T(8,128)S(1)}, f32[3,1024]{1,0:T(4,128)S(1)}, f32[2,6,2048]{2,1,0:T(8,128)S(1)}, f32[3,1024]{1,0:T(4,128)S(1)},...) while((s32[]{:T(128)}, f32[2,6,2048]{2,1,0:T(8,128)S(1)}, ...), condition=%wide.region_35.36_spmd, body=%wide.region_28.35_spmd.sunk | while | flops 85970952 | bytes 499925 | solution.py:37
  363.4 16.2 fusion.191
  379.9 16.2 fusion.191
  396.2 1.4 gather_fusion.1
  397.6 1.9 scatter_fusion.1
  399.8 97.2 %gather_fusion.15 = s32[16384]{0:T(1024)S(1)} fusion(s32[128]{0:T(128)S(1)} %get-tuple-element.733, s32[16384]{0:T(1024)S(1)} %broadcast_clamp_fusion.2), kind=kCustom, calls=%fused_computation.15 | custom fusion | bytes 196608 | tf_op jit(solution)/shard_map/gather | solution.py:84
  497.1 1.4 gather_fusion.10
  509.3 137.8 %all-reduce.11.cloned.1.call-done = f32[6,4096]{1,0:T(8,128)} async-done(((f32[6,4096]{1,0:T(8,128)}), f32[6,4096]{1,0:T(8,128)}) %all-reduce.11.cloned.1.call-update) | async-done | bytes 98320 | tf_op jit(solution)/shard_map/psum | solution.py:96
  647.2 0.9 constant_dynamic-update-slice_fusion.3
  648.1 141.3 %all-reduce.13.cloned.1.call-done = f32[6,4096]{1,0:T(8,128)} async-done(((f32[6,4096]{1,0:T(8,128)}), f32[6,4096]{1,0:T(8,128)}) %all-reduce.13.cloned.1.call-update) | async-done | bytes 98320 | tf_op jit(solution)/shard_map/psum | solution.py:96
  789.5 0.9 constant_dynamic-update-slice_fusion.2
  790.4 141.8 %all-reduce.15.cloned.1.call-done = f32[6,4096]{1,0:T(8,128)} async-done(((f32[6,4096]{1,0:T(8,128)}), f32[6,4096]{1,0:T(8,128)}) %all-reduce.15.cloned.1.call-update) | async-done | bytes 98320 | tf_op jit(solution)/shard_map/psum | solution.py:96
  933.4 1.4 scatter_fusion
  934.9 1.4 scatter_fusion.3
  936.4 1.4 scatter_fusion.2
  937.9 1.4 scatter_fusion.4
  941.9 59.0 %all-gather.3 = f32[128,6,256]{2,1,0:T(8,128)S(1)} all-gather(f32[1,6,256]{2,1,0:T(8,128)S(1)} %maximum_bitcast_fusion.1), channel_id=3, replica_groups=mesh['grp'=8,'dev'=16] {'grp','dev'}, dimensions={0}, use_global_device_ids=true | all-gather | bytes 792576 | tf_op jit(solution)/shard_map/all_gather | solution.py:85
  1000.9 8.4 copy.274
  1009.3 60.2 %gather_fusion.16 = f32[16384,6]{1,0:T(8,128)} fusion(f32[6,32768]{0,1:T(8,128)} %bitcast.633, s32[16384]{0:T(1024)S(1)} %broadcast_clamp_fusion), kind=kCustom, calls=%fused_computation.16 | custom fusion | bytes 851968 | tf_op jit(solution)/shard_map/gather | solution.py:87
  1069.4 6.2 fusion.166
  1075.6 2.2 copy.276
  1077.9 32.8 %while.84 = (s32[]{:T(128)}, f32[2,6,2048]{2,1,0:T(8,128)S(1)}, f32[3,1024]{1,0:T(4,128)S(1)}, f32[2,6,2048]{2,1,0:T(8,128)S(1)}, f32[3,1024]{1,0:T(4,128)S(1)},...) while((s32[]{:T(128)}, f32[2,6,2048]{2,1,0:T(8,128)S(1)}, ...), condition=%wide.region_52.53_spmd, body=%wide.region_45.52_spmd.sunk | while | flops 85970952 | bytes 499925 | solution.py:37
  1078.0 16.2 fusion.193
  1094.4 16.2 fusion.193
  1110.7 2.3 copy.279
  1113.6 34.0 %while.85 = (s32[]{:T(128)}, f32[2,6,2048]{2,1,0:T(8,128)}, f32[3,1024]{1,0:T(4,128)S(1)}, f32[2,6,2048]{2,1,0:T(8,128)S(1)}, f32[3,1024]{1,0:T(4,128)S(1)}, /*i...) while((s32[]{:T(128)}, f32[2,6,2048]{2,1,0:T(8,128)}, f32[3,1024]{1,0:T(4,128)S(1)}, ...), condition=%wide.region_60.61_spmd, body=%wide.region_53.60_spmd.sunk | while | flops 85970952 | bytes 483541 | solution.py:37
  1113.7 16.2 fusion.195
  1130.7 16.2 fusion.195
  1147.9 2.2 copy.282
  1150.1 32.8 %while.86 = (s32[]{:T(128)}, f32[2,6,2048]{2,1,0:T(8,128)S(1)}, f32[3,1024]{1,0:T(4,128)S(1)}, f32[2,6,2048]{2,1,0:T(8,128)S(1)}, f32[3,1024]{1,0:T(4,128)S(1)},...) while((s32[]{:T(128)}, f32[2,6,2048]{2,1,0:T(8,128)S(1)}, ...), condition=%wide.region_69.70_spmd, body=%wide.region_62.69_spmd.sunk | while | flops 85970952 | bytes 499925 | solution.py:37
  1150.2 16.2 fusion.197
  1166.6 16.2 fusion.197
  1183.7 32.8 %while.87 = (s32[]{:T(128)}, f32[2,6,2048]{2,1,0:T(8,128)S(1)}, f32[3,1024]{1,0:T(4,128)S(1)}, f32[2,6,2048]{2,1,0:T(8,128)S(1)}, f32[3,1024]{1,0:T(4,128)S(1)},...) while((s32[]{:T(128)}, f32[2,6,2048]{2,1,0:T(8,128)S(1)}, ...), condition=%wide.region_78.79_spmd, body=%wide.region_71.78_spmd.sunk | while | flops 85970952 | bytes 499925 | solution.py:37
  1183.8 16.2 fusion.199
  1200.2 16.2 fusion.199
  1219.8 66.7 %all-reduce.17.cloned.1.call-done = f32[6,4096]{1,0:T(8,128)} async-done(((f32[6,4096]{1,0:T(8,128)}), f32[6,4096]{1,0:T(8,128)}) %all-reduce.17.cloned.1.call-update) | async-done | bytes 98320 | tf_op jit(solution)/shard_map/psum | solution.py:96
  1287.5 141.8 %all-reduce.19.cloned.1.call-done = f32[6,4096]{1,0:T(8,128)} async-done(((f32[6,4096]{1,0:T(8,128)}), f32[6,4096]{1,0:T(8,128)}) %all-reduce.19.cloned.1.call-update) | async-done | bytes 98320 | tf_op jit(solution)/shard_map/psum | solution.py:96
  1430.3 141.2 %all-reduce.21.cloned.1.call-done = f32[6,4096]{1,0:T(8,128)} async-done(((f32[6,4096]{1,0:T(8,128)}), f32[6,4096]{1,0:T(8,128)}) %all-reduce.21.cloned.1.call-update) | async-done | bytes 98320 | tf_op jit(solution)/shard_map/psum | solution.py:96
  1571.5 0.9 constant_dynamic-update-slice_fusion.7
  1572.5 142.0 %all-reduce.23.cloned.1.call-done = f32[6,4096]{1,0:T(8,128)} async-done(((f32[6,4096]{1,0:T(8,128)}), f32[6,4096]{1,0:T(8,128)}) %all-reduce.23.cloned.1.call-update) | async-done | bytes 98320 | tf_op jit(solution)/shard_map/psum | solution.py:96
  1715.6 1.4 scatter_fusion.5
  1717.9 1.4 scatter_fusion.6
  1720.2 1.4 scatter_fusion.7
  1722.6 1.4 scatter_fusion.8
  (218 shorter events, 34.7 us)
Async XLA Ops:
  7.2 501.2 %all-reduce.9.cloned.1.call-start = ((), (), s32[]{:S(2)}) async-start(), calls=%async_computation | async-start | bytes 262144 | tf_op jit(solution)/shard_map/psum | solution.py:96
  78.7 11.5 copy-start.18
  289.1 0.6 copy-start.5
  289.8 357.4 %all-reduce.11.cloned.1.call-start = ((), (), s32[]{:S(2)}) async-start(), calls=%async_computation.1 | async-start | bytes 262144 | tf_op jit(solution)/shard_map/psum | solution.py:96
  327.5 2.3 copy-start.6
  362.7 0.7 copy-start.7
  396.2 100.8 %copy-start.8 = (f32[2,6,2048]{2,1,0:T(8,128)}, f32[2,6,2048]{2,1,0:T(8,128)S(1)}, u32[]{:S(2)}) copy-start(f32[2,6,2048]{2,1,0:T(8,128)S(1)} %get-tuple-element.238) | copy-start | bytes 294916
  397.6 543.1 %copy-start.15 = (s32[1024]{0:T(1024)}, s32[1024]{0:T(1024)S(1)}, u32[]{:S(2)}) copy-start(s32[1024]{0:T(1024)S(1)} %pad_clamp_fusion) | copy-start | bytes 12292
  399.7 99.4 %copy-start.11 = (f32[3,1024]{1,0:T(4,128)S(1)}, f32[3,1024]{1,0:T(4,128)}, u32[]{:S(2)}) copy-start(f32[3,1024]{1,0:T(4,128)} %param.23) | copy-start | bytes 36868
  399.7 99.6 %copy-start.12 = (f32[3,1024]{1,0:T(4,128)S(1)}, f32[3,1024]{1,0:T(4,128)}, u32[]{:S(2)}) copy-start(f32[3,1024]{1,0:T(4,128)} %param.25) | copy-start | bytes 36868
  399.7 99.8 %copy-start.13 = (f32[3,1024]{1,0:T(4,128)S(1)}, f32[3,1024]{1,0:T(4,128)}, u32[]{:S(2)}) copy-start(f32[3,1024]{1,0:T(4,128)} %param.24) | copy-start | bytes 36868
  399.7 100.7 %copy-start.14 = (f32[3,1024]{1,0:T(4,128)S(1)}, f32[3,1024]{1,0:T(4,128)}, u32[]{:S(2)}) copy-start(f32[3,1024]{1,0:T(4,128)} %param.26) | copy-start | bytes 36868
  508.4 281.0 %all-reduce.13.cloned.1.call-start = ((), (), s32[]{:S(2)}) async-start(), calls=%async_computation.2 | async-start | bytes 262144 | tf_op jit(solution)/shard_map/psum | solution.py:96
  647.2 285.0 %all-reduce.15.cloned.1.call-start = ((), (), s32[]{:S(2)}) async-start(), calls=%async_computation.3 | async-start | bytes 262144 | tf_op jit(solution)/shard_map/psum | solution.py:96
  789.4 497.1 %all-reduce.17.cloned.1.call-start = ((), (), s32[]{:S(2)}) async-start(), calls=%async_computation.4 | async-start | bytes 262144 | tf_op jit(solution)/shard_map/psum | solution.py:96
  934.7 74.5 %copy-start.2 = (f32[3,1024]{0,1:T(8,128)}, f32[3,1024]{0,1:T(8,128)S(1)}, u32[]{:S(2)}) copy-start(f32[3,1024]{0,1:T(8,128)S(1)} %scatter_fusion) | copy-start | bytes 36868
  936.3 73.0 %copy-start = (f32[3,1024]{0,1:T(8,128)}, f32[3,1024]{0,1:T(8,128)S(1)}, u32[]{:S(2)}) copy-start(f32[3,1024]{0,1:T(8,128)S(1)} %scatter_fusion.3) | copy-start | bytes 36868
  1110.7 2.9 copy-start.9
  1147.6 281.7 %all-reduce.19.cloned.1.call-start = ((), (), s32[]{:S(2)}) async-start(), calls=%async_computation.5 | async-start | bytes 262144 | tf_op jit(solution)/shard_map/psum | solution.py:96
  1183.0 0.7 copy-start.10
  1183.6 32.9 %copy-start.1 = (f32[3,1024]{0,1:T(8,128)S(1)}, f32[3,1024]{0,1:T(8,128)}, u32[]{:S(2)}) copy-start(f32[3,1024]{0,1:T(8,128)} %copy-done) | copy-start | bytes 36868
  1183.6 32.9 %copy-start.16 = (s32[1024]{0:T(1024)S(1)}, s32[1024]{0:T(1024)}, u32[]{:S(2)}) copy-start(s32[1024]{0:T(1024)} %copy-done.15) | copy-start | bytes 12292
  1183.6 34.3 %copy-start.3 = (f32[3,1024]{0,1:T(8,128)S(1)}, f32[3,1024]{0,1:T(8,128)}, u32[]{:S(2)}) copy-start(f32[3,1024]{0,1:T(8,128)} %copy-done.2) | copy-start | bytes 36868
  1183.6 531.7 %copy-start.19 = (f32[256]{0:T(256)S(1)}, f32[256]{0:T(256)}, u32[]{:S(2)}) copy-start(f32[256]{0:T(256)} %get-tuple-element.731) | copy-start | bytes 3076
  1183.6 531.7 %copy-start.20 = (f32[256]{0:T(256)S(1)}, f32[256]{0:T(256)}, u32[]{:S(2)}) copy-start(f32[256]{0:T(256)} %get-tuple-element.732) | copy-start | bytes 3076
  1183.7 531.9 %copy-start.17 = (s32[256,1]{0,1:T(1,128)S(1)}, s32[256,1]{0,1:T(1,128)}, u32[]{:S(2)}) copy-start(s32[256,1]{0,1:T(1,128)} %get-tuple-element.729) | copy-start | bytes 3076
  1216.5 355.0 %copy-start.4 = (f32[2,6,2048]{2,1,0:T(8,128)}, f32[2,6,2048]{2,1,0:T(8,128)S(1)}, u32[]{:S(2)}) copy-start(f32[2,6,2048]{2,1,0:T(8,128)S(1)} %get-tuple-element.248) | copy-start | bytes 294916
  1286.5 285.0 %all-reduce.21.cloned.1.call-start = ((), (), s32[]{:S(2)}) async-start(), calls=%async_computation.6 | async-start | bytes 262144 | tf_op jit(solution)/shard_map/psum | solution.py:96
  1429.3 285.1 %all-reduce.23.cloned.1.call-start = ((), (), s32[]{:S(2)}) async-start(), calls=%async_computation.7 | async-start | bytes 262144 | tf_op jit(solution)/shard_map/psum | solution.py:96
Sparse Core Ops, SparseCore 0:
  289.9 138.5 all-reduce.8
  508.5 138.5 all-reduce.10
  651.9 137.4 all-reduce.12
  794.7 137.4 all-reduce.14
  1147.8 138.6 all-reduce.16
  1291.8 137.4 all-reduce.18
  1434.0 137.4 all-reduce.20
  1577.0 137.4 all-reduce.22
where the time goes:
time: 1740 us; the launch traced here: 1730 us
  waiting for transfers between devices  913 us (52%)
  local copies, waits for them, and re-layouts  405 us (23%)
  other arithmetic  270 us (16%)
  blocking collectives  123 us (7%)
  between operations  19 us (1%)
    psum x8, waiting for transfers between devices, shards(): summed = lax.psum(terms, ('grp', 'dev'))  913 us
    reduce_sum x16, other arithmetic, pair_block(): jnp.sum(weight * (drift_z - along * gap_z), axis=1)  259 us
    gather x2, local copies, waits for them, and re-layouts, shards(): slot = owner * slot_cap + place - first[owner]  194 us
    all_gather x2, blocking collectives, shards(): gathered = lax.all_gather(targets[None], ('grp', 'dev'), axis=0, tiled=True)  123 us
    gather x2, local copies, waits for them, and re-layouts, shards(): compact = flat[:, slot]  120 us
  transfers between devices with their start and end apart: 8, of which 7 were waited for; matrix products, arithmetic and copies ran while one was open for 17% of the time, Pallas kernels for 0%

commit v1 on v0

--- a/solution.py
+++ b/solution.py
@@ -3,8 +3,13 @@
 import jax.numpy as jnp
 from jax import lax
 from jax.sharding import PartitionSpec as P
+from jax.lax import all_gather
 
 tick_length = 1.0 / 128.0
+
+
+def touch_column(values):
+    return jnp.sum(all_gather(values, ("grp", "dev")), axis=0)
 
 
 def pair_block(targets, src_pos, src_vel, mass, soft_sq):
@@ -93,7 +98,7 @@
             if summed is not None:
                 terms, summed = lax.optimization_barrier((terms, summed))
                 parts.append(summed)
-            summed = lax.psum(terms, ("grp", "dev"))
+            summed = touch_column(terms)
         parts.append(summed)
         parts.append(jnp.zeros((6, slot_cap), jnp.float32))
         totals = jnp.concatenate(parts, axis=1)

time: 1740 us -> 1220 us (0.70)
  waiting for transfers between devices: 913 us -> 336 us
  other arithmetic: 270 us -> 330 us
    psum x8 -> x0, waiting for transfers between devices: 913 us -> none  [shards(): summed = lax.psum(terms, ('grp', 'dev'))]
    all_gather x0 -> x8, waiting for transfers between devices: none -> 336 us  [touch_column(): return jnp.sum(all_gather(values, ('grp', 'dev')), axis=0)]
    reduce_sum x0 -> x8, other arithmetic: none -> 56.1 us  [touch_column(): return jnp.sum(all_gather(values, ('grp', 'dev')), axis=0)]
  transfers between devices with their start and end apart: 8 -> 8, of which waited for: 7 -> 7; matrix products, arithmetic and copies ran while one was open for 17% -> 27% of each run, Pallas kernels for 0% -> 0%
where the time goes in v1:
time: 1220 us; the launch traced here: 1210 us
  local copies, waits for them, and re-layouts  403 us (33%)
  waiting for transfers between devices  336 us (28%)
  other arithmetic  330 us (27%)
  blocking collectives  124 us (10%)
  between operations  19.1 us (2%)
    all_gather x8, waiting for transfers between devices, touch_column(): return jnp.sum(all_gather(values, ('grp', 'dev')), axis=0)  336 us
    reduce_sum x16, other arithmetic, pair_block(): jnp.sum(weight * (drift_z - along * gap_z), axis=1)  263 us
    gather x2, local copies, waits for them, and re-layouts, shards(): slot = owner * slot_cap + place - first[owner]  194 us
    all_gather x2, blocking collectives, shards(): gathered = lax.all_gather(targets[None], ('grp', 'dev'), axis=0, tiled=True)  124 us
    gather x2, local copies, waits for them, and re-layouts, shards(): compact = flat[:, slot]  120 us
    reduce_sum x8, other arithmetic, touch_column(): return jnp.sum(all_gather(values, ('grp', 'dev')), axis=0)  56.1 us
  transfers between devices with their start and end apart: 8, of which 7 were waited for; matrix products, arithmetic and copies ran while one was open for 27% of the time, Pallas kernels for 0%

profile of v1, /device:TPU:1, one launch (start us, length us, event | category | flops | bytes accessed | tf_op | source)
XLA Modules:
  0.0 1213.6 jit_solution(15277183723688861052)
XLA Ops:
  8.6 2.6 compare_select_fusion.4
  14.8 63.9 %all-gather.8 = f32[128,6,256]{2,1,0:T(8,128)S(1)} all-gather(f32[1,6,256]{2,1,0:T(8,128)S(1)} %maximum_bitcast_fusion), channel_id=2, replica_groups=mesh['grp'=8,'dev'=16] {'grp','dev'}, dimensions={0}, use_global_device_ids=true | all-gather | bytes 792576 | tf_op jit(solution)/shard_map/all_gather | solution.py:90
  78.7 8.4 copy.237
  87.8 2.3 convert_reduce_fusion.1
  90.3 97.2 %gather_fusion.6 = s32[16384]{0:T(1024)S(1)} fusion(s32[128]{0:T(128)S(1)} %get-tuple-element.734, s32[16384]{0:T(1024)S(1)} %broadcast_clamp_fusion.3), kind=kCustom, calls=%fused_computation.6 | custom fusion | bytes 196608 | tf_op jit(solution)/shard_map/gather | solution.py:89
  187.7 60.2 %gather_fusion.7 = f32[16384,6]{1,0:T(8,128)} fusion(f32[6,32768]{0,1:T(8,128)} %bitcast.638, s32[16384]{0:T(1024)S(1)} %broadcast_clamp_fusion.1), kind=kCustom, calls=%fused_computation.7 | custom fusion | bytes 851968 | tf_op jit(solution)/shard_map/gather | solution.py:92
  247.9 6.2 fusion.167
  254.1 2.2 copy.240
  256.3 32.9 %while.81 = (s32[]{:T(128)}, f32[2,6,2048]{2,1,0:T(8,128)S(1)}, f32[3,1024]{1,0:T(4,128)S(1)}, f32[2,6,2048]{2,1,0:T(8,128)S(1)}, f32[3,1024]{1,0:T(4,128)S(1)},...) while((s32[]{:T(128)}, f32[2,6,2048]{2,1,0:T(8,128)S(1)}, ...), condition=%wide.region_17.18_spmd, body=%wide.region_10.17_spmd.sunk | while | flops 85970952 | bytes 499925 | solution.py:42
  256.4 16.2 %fusion.187 = (f32[2048]{0:T(1024)S(1)}, f32[2048]{0:T(1024)S(1)}, f32[2048]{0:T(1024)S(1)}, f32[2048]{0:T(1024)S(1)}, f32[2048]{0:T(1024)S(1)}, /*index=5*/f32[2048]{0:T(1024)S(1)}) fusion(f32[2048]{0:T(1024)S(1)} %bitcast.731, f32[1024]{0:T(1024)S(1)} %bitcast.779, f32[2048]{0:T(1024)S(1)} %bitcast.728, f32[1024]{0:T(1024)S(1)} %bitcast.782, ...), kind=kLoop, calls=%fused_computation.89.clone.1 | loop fusion | flops 85970944 | bytes 122880 | tf_op jit(solution)/shard_map/while/body/eval_jaxpr/reduce_sum | solution.py:33
  272.8 16.2 %fusion.187 = (f32[2048]{0:T(1024)S(1)}, f32[2048]{0:T(1024)S(1)}, f32[2048]{0:T(1024)S(1)}, f32[2048]{0:T(1024)S(1)}, f32[2048]{0:T(1024)S(1)}, /*index=5*/f32[2048]{0:T(1024)S(1)}) fusion(f32[2048]{0:T(1024)S(1)} %bitcast.731, f32[1024]{0:T(1024)S(1)} %bitcast.779, f32[2048]{0:T(1024)S(1)} %bitcast.728, f32[1024]{0:T(1024)S(1)} %bitcast.782, ...), kind=kLoop, calls=%fused_computation.89.clone.1 | loop fusion | flops 85970944 | bytes 122880 | tf_op jit(solution)/shard_map/while/body/eval_jaxpr/reduce_sum | solution.py:33
  290.1 2.2 copy.239
  292.3 32.9 %while.80 = (s32[]{:T(128)}, f32[2,6,2048]{2,1,0:T(8,128)S(1)}, f32[3,1024]{1,0:T(4,128)S(1)}, f32[2,6,2048]{2,1,0:T(8,128)S(1)}, f32[3,1024]{1,0:T(4,128)S(1)},...) while((s32[]{:T(128)}, f32[2,6,2048]{2,1,0:T(8,128)S(1)}, ...), condition=%wide.region_9.10_spmd, body=%wide.region_2.9_spmd.sunk | while | flops 85970952 | bytes 499925 | solution.py:42
  292.4 16.2 %fusion.185 = (f32[2048]{0:T(1024)S(1)}, f32[2048]{0:T(1024)S(1)}, f32[2048]{0:T(1024)S(1)}, f32[2048]{0:T(1024)S(1)}, f32[2048]{0:T(1024)S(1)}, /*index=5*/f32[2048]{0:T(1024)S(1)}) fusion(f32[2048]{0:T(1024)S(1)} %bitcast.737, f32[1024]{0:T(1024)S(1)} %bitcast.785, f32[2048]{0:T(1024)S(1)} %bitcast.734, f32[1024]{0:T(1024)S(1)} %bitcast.788, ...), kind=kLoop, calls=%fused_computation.49.clone.1 | loop fusion | flops 85970944 | bytes 122880 | tf_op jit(solution)/shard_map/while/body/eval_jaxpr/reduce_sum | solution.py:33
  308.8 16.2 %fusion.185 = (f32[2048]{0:T(1024)S(1)}, f32[2048]{0:T(1024)S(1)}, f32[2048]{0:T(1024)S(1)}, f32[2048]{0:T(1024)S(1)}, f32[2048]{0:T(1024)S(1)}, /*index=5*/f32[2048]{0:T(1024)S(1)}) fusion(f32[2048]{0:T(1024)S(1)} %bitcast.737, f32[1024]{0:T(1024)S(1)} %bitcast.785, f32[2048]{0:T(1024)S(1)} %bitcast.734, f32[1024]{0:T(1024)S(1)} %bitcast.788, ...), kind=kLoop, calls=%fused_computation.49.clone.1 | loop fusion | flops 85970944 | bytes 122880 | tf_op jit(solution)/shard_map/while/body/eval_jaxpr/reduce_sum | solution.py:33
  325.2 44.1 %all-gather.25.cloned.1.call-done = f32[128,6,4096]{2,1,0:T(8,128)} async-done(((f32[1,6,4096]{2,1,0:T(8,128)}), f32[128,6,4096]{2,1,0:T(8,128)}) %all-gather.25.cloned.1.call-update) | async-done | bytes 12582928 | tf_op jit(solution)/shard_map/all_gather | solution.py:12
  369.3 6.9 reduce_sum.523
  376.3 2.2 copy.241
  378.5 32.9 %while.82 = (s32[]{:T(128)}, f32[2,6,2048]{2,1,0:T(8,128)S(1)}, f32[3,1024]{1,0:T(4,128)S(1)}, f32[2,6,2048]{2,1,0:T(8,128)S(1)}, f32[3,1024]{1,0:T(4,128)S(1)},...) while((s32[]{:T(128)}, f32[2,6,2048]{2,1,0:T(8,128)S(1)}, ...), condition=%wide.region_26.27_spmd, body=%wide.region_19.26_spmd.sunk | while | flops 85970952 | bytes 499925 | solution.py:42
  378.6 16.2 %fusion.189 = (f32[2048]{0:T(1024)S(1)}, f32[2048]{0:T(1024)S(1)}, f32[2048]{0:T(1024)S(1)}, f32[2048]{0:T(1024)S(1)}, f32[2048]{0:T(1024)S(1)}, /*index=5*/f32[2048]{0:T(1024)S(1)}) fusion(f32[2048]{0:T(1024)S(1)} %bitcast.743, f32[1024]{0:T(1024)S(1)} %bitcast.791, f32[2048]{0:T(1024)S(1)} %bitcast.740, f32[1024]{0:T(1024)S(1)} %bitcast.794, ...), kind=kLoop, calls=%fused_computation.129.clone.1 | loop fusion | flops 85970944 | bytes 122880 | tf_op jit(solution)/shard_map/while/body/eval_jaxpr/reduce_sum | solution.py:33
  395.1 16.2 %fusion.189 = (f32[2048]{0:T(1024)S(1)}, f32[2048]{0:T(1024)S(1)}, f32[2048]{0:T(1024)S(1)}, f32[2048]{0:T(1024)S(1)}, f32[2048]{0:T(1024)S(1)}, /*index=5*/f32[2048]{0:T(1024)S(1)}) fusion(f32[2048]{0:T(1024)S(1)} %bitcast.743, f32[1024]{0:T(1024)S(1)} %bitcast.791, f32[2048]{0:T(1024)S(1)} %bitcast.740, f32[1024]{0:T(1024)S(1)} %bitcast.794, ...), kind=kLoop, calls=%fused_computation.129.clone.1 | loop fusion | flops 85970944 | bytes 122880 | tf_op jit(solution)/shard_map/while/body/eval_jaxpr/reduce_sum | solution.py:33
  411.4 44.8 %all-gather.29.cloned.1.call-done = f32[128,6,4096]{2,1,0:T(8,128)} async-done(((f32[1,6,4096]{2,1,0:T(8,128)}), f32[128,6,4096]{2,1,0:T(8,128)}) %all-gather.29.cloned.1.call-update) | async-done | bytes 12582928 | tf_op jit(solution)/shard_map/all_gather | solution.py:12
  456.2 6.9 reduce_sum.524
  463.9 32.9 %while.83 = (s32[]{:T(128)}, f32[2,6,2048]{2,1,0:T(8,128)S(1)}, f32[3,1024]{1,0:T(4,128)S(1)}, f32[2,6,2048]{2,1,0:T(8,128)S(1)}, f32[3,1024]{1,0:T(4,128)S(1)},...) while((s32[]{:T(128)}, f32[2,6,2048]{2,1,0:T(8,128)S(1)}, ...), condition=%wide.region_35.36_spmd, body=%wide.region_28.35_spmd.sunk | while | flops 85970952 | bytes 499925 | solution.py:42
  464.0 16.2 %fusion.191 = (f32[2048]{0:T(1024)S(1)}, f32[2048]{0:T(1024)S(1)}, f32[2048]{0:T(1024)S(1)}, f32[2048]{0:T(1024)S(1)}, f32[2048]{0:T(1024)S(1)}, /*index=5*/f32[2048]{0:T(1024)S(1)}) fusion(f32[2048]{0:T(1024)S(1)} %bitcast.749, f32[1024]{0:T(1024)S(1)} %bitcast.797, f32[2048]{0:T(1024)S(1)} %bitcast.746, f32[1024]{0:T(1024)S(1)} %bitcast.800, ...), kind=kLoop, calls=%fused_computation.169.clone.1 | loop fusion | flops 85970944 | bytes 122880 | tf_op jit(solution)/shard_map/while/body/eval_jaxpr/reduce_sum | solution.py:33
  480.4 16.2 %fusion.191 = (f32[2048]{0:T(1024)S(1)}, f32[2048]{0:T(1024)S(1)}, f32[2048]{0:T(1024)S(1)}, f32[2048]{0:T(1024)S(1)}, f32[2048]{0:T(1024)S(1)}, /*index=5*/f32[2048]{0:T(1024)S(1)}) fusion(f32[2048]{0:T(1024)S(1)} %bitcast.749, f32[1024]{0:T(1024)S(1)} %bitcast.797, f32[2048]{0:T(1024)S(1)} %bitcast.746, f32[1024]{0:T(1024)S(1)} %bitcast.800, ...), kind=kLoop, calls=%fused_computation.169.clone.1 | loop fusion | flops 85970944 | bytes 122880 | tf_op jit(solution)/shard_map/while/body/eval_jaxpr/reduce_sum | solution.py:33
  496.8 46.4 %all-gather.31.cloned.1.call-done = f32[128,6,4096]{2,1,0:T(8,128)} async-done(((f32[1,6,4096]{2,1,0:T(8,128)}), f32[128,6,4096]{2,1,0:T(8,128)}) %all-gather.31.cloned.1.call-update) | async-done | bytes 12582928 | tf_op jit(solution)/shard_map/all_gather | solution.py:12
  543.2 6.9 reduce_sum.525
  558.5 2.3 convert_reduce_fusion
  561.0 97.2 %gather_fusion.15 = s32[16384]{0:T(1024)S(1)} fusion(s32[128]{0:T(128)S(1)} %get-tuple-element.733, s32[16384]{0:T(1024)S(1)} %broadcast_clamp_fusion.2), kind=kCustom, calls=%fused_computation.15 | custom fusion | bytes 196608 | tf_op jit(solution)/shard_map/gather | solution.py:89
  658.2 1.4 scatter_fusion.1
  659.9 6.9 reduce_sum.526
  667.1 1.4 scatter_fusion
  668.6 1.4 scatter_fusion.3
  670.2 1.4 scatter_fusion.2
  671.7 1.4 scatter_fusion.4
  675.6 60.3 %all-gather.12 = f32[128,6,256]{2,1,0:T(8,128)S(1)} all-gather(f32[1,6,256]{2,1,0:T(8,128)S(1)} %maximum_bitcast_fusion.1), channel_id=6, replica_groups=mesh['grp'=8,'dev'=16] {'grp','dev'}, dimensions={0}, use_global_device_ids=true | all-gather | bytes 792576 | tf_op jit(solution)/shard_map/all_gather | solution.py:90
  735.9 8.4 copy.258
  744.3 60.2 %gather_fusion.16 = f32[16384,6]{1,0:T(8,128)} fusion(f32[6,32768]{0,1:T(8,128)} %bitcast.639, s32[16384]{0:T(1024)S(1)} %broadcast_clamp_fusion), kind=kCustom, calls=%fused_computation.16 | custom fusion | bytes 851968 | tf_op jit(solution)/shard_map/gather | solution.py:92
  804.4 6.2 fusion.166
  810.6 2.2 copy.263
  812.9 35.4 %while.85 = (s32[]{:T(128)}, f32[2,6,2048]{2,1,0:T(8,128)S(1)}, f32[3,1024]{1,0:T(4,128)S(1)}, f32[2,6,2048]{2,1,0:T(8,128)S(1)}, f32[3,1024]{1,0:T(4,128)S(1)},...) while((s32[]{:T(128)}, f32[2,6,2048]{2,1,0:T(8,128)S(1)}, ...), condition=%wide.region_60.61_spmd, body=%wide.region_53.60_spmd.sunk | while | flops 85970952 | bytes 499925 | solution.py:42
  813.0 16.8 %fusion.195 = (f32[2048]{0:T(1024)S(1)}, f32[2048]{0:T(1024)S(1)}, f32[2048]{0:T(1024)S(1)}, f32[2048]{0:T(1024)S(1)}, f32[2048]{0:T(1024)S(1)}, /*index=5*/f32[2048]{0:T(1024)}) fusion(f32[2048]{0:T(1024)S(1)} %bitcast.755, f32[1024]{0:T(1024)S(1)} %bitcast.803, f32[2048]{0:T(1024)S(1)} %bitcast.752, f32[1024]{0:T(1024)S(1)} %bitcast.806, ...), kind=kLoop, calls=%fused_computation.249.clone.1 | loop fusion | flops 85970944 | bytes 122880 | tf_op jit(solution)/shard_map/while/body/eval_jaxpr/reduce_sum | solution.py:33
  830.7 16.8 %fusion.195 = (f32[2048]{0:T(1024)S(1)}, f32[2048]{0:T(1024)S(1)}, f32[2048]{0:T(1024)S(1)}, f32[2048]{0:T(1024)S(1)}, f32[2048]{0:T(1024)S(1)}, /*index=5*/f32[2048]{0:T(1024)}) fusion(f32[2048]{0:T(1024)S(1)} %bitcast.755, f32[1024]{0:T(1024)S(1)} %bitcast.803, f32[2048]{0:T(1024)S(1)} %bitcast.752, f32[1024]{0:T(1024)S(1)} %bitcast.806, ...), kind=kLoop, calls=%fused_computation.249.clone.1 | loop fusion | flops 85970944 | bytes 122880 | tf_op jit(solution)/shard_map/while/body/eval_jaxpr/reduce_sum | solution.py:33
  849.0 2.2 copy.260
  851.2 35.4 %while.84 = (s32[]{:T(128)}, f32[2,6,2048]{2,1,0:T(8,128)S(1)}, f32[3,1024]{1,0:T(4,128)S(1)}, f32[2,6,2048]{2,1,0:T(8,128)S(1)}, f32[3,1024]{1,0:T(4,128)S(1)},...) while((s32[]{:T(128)}, f32[2,6,2048]{2,1,0:T(8,128)S(1)}, ...), condition=%wide.region_52.53_spmd, body=%wide.region_45.52_spmd.sunk | while | flops 85970952 | bytes 499925 | solution.py:42
  851.3 16.8 %fusion.193 = (f32[2048]{0:T(1024)S(1)}, f32[2048]{0:T(1024)S(1)}, f32[2048]{0:T(1024)S(1)}, f32[2048]{0:T(1024)S(1)}, f32[2048]{0:T(1024)S(1)}, /*index=5*/f32[2048]{0:T(1024)}) fusion(f32[2048]{0:T(1024)S(1)} %bitcast.761, f32[1024]{0:T(1024)S(1)} %bitcast.809, f32[2048]{0:T(1024)S(1)} %bitcast.758, f32[1024]{0:T(1024)S(1)} %bitcast.812, ...), kind=kLoop, calls=%fused_computation.209.clone.1 | loop fusion | flops 85970944 | bytes 122880 | tf_op jit(solution)/shard_map/while/body/eval_jaxpr/reduce_sum | solution.py:33
  869.0 16.8 %fusion.193 = (f32[2048]{0:T(1024)S(1)}, f32[2048]{0:T(1024)S(1)}, f32[2048]{0:T(1024)S(1)}, f32[2048]{0:T(1024)S(1)}, f32[2048]{0:T(1024)S(1)}, /*index=5*/f32[2048]{0:T(1024)}) fusion(f32[2048]{0:T(1024)S(1)} %bitcast.761, f32[1024]{0:T(1024)S(1)} %bitcast.809, f32[2048]{0:T(1024)S(1)} %bitcast.758, f32[1024]{0:T(1024)S(1)} %bitcast.812, ...), kind=kLoop, calls=%fused_computation.209.clone.1 | loop fusion | flops 85970944 | bytes 122880 | tf_op jit(solution)/shard_map/while/body/eval_jaxpr/reduce_sum | solution.py:33
  887.3 41.5 %all-gather.27.cloned.1.call-done = f32[128,6,4096]{2,1,0:T(8,128)} async-done(((f32[1,6,4096]{2,1,0:T(8,128)}), f32[128,6,4096]{2,1,0:T(8,128)}) %all-gather.27.cloned.1.call-update) | async-done | bytes 12582928 | tf_op jit(solution)/shard_map/all_gather | solution.py:12
  928.8 6.9 reduce_sum.528
  936.0 2.2 copy.266
  938.9 36.6 %while.86 = (s32[]{:T(128)}, f32[2,6,2048]{2,1,0:T(8,128)}, f32[3,1024]{1,0:T(4,128)S(1)}, f32[2,6,2048]{2,1,0:T(8,128)S(1)}, f32[3,1024]{1,0:T(4,128)S(1)}, /*i...) while((s32[]{:T(128)}, f32[2,6,2048]{2,1,0:T(8,128)}, f32[3,1024]{1,0:T(4,128)S(1)}, ...), condition=%wide.region_69.70_spmd, body=%wide.region_62.69_spmd.sunk | while | flops 85970952 | bytes 483541 | solution.py:42
  939.0 16.8 %fusion.197 = (f32[2048]{0:T(1024)S(1)}, f32[2048]{0:T(1024)S(1)}, f32[2048]{0:T(1024)S(1)}, f32[2048]{0:T(1024)S(1)}, f32[2048]{0:T(1024)S(1)}, /*index=5*/f32[2048]{0:T(1024)}) fusion(f32[2048]{0:T(1024)S(1)} %bitcast.767, f32[1024]{0:T(1024)S(1)} %bitcast.815, f32[2048]{0:T(1024)S(1)} %bitcast.764, f32[1024]{0:T(1024)S(1)} %bitcast.818, ...), kind=kLoop, calls=%fused_computation.289.clone.1 | loop fusion | flops 85970944 | bytes 122880 | tf_op jit(solution)/shard_map/while/body/eval_jaxpr/reduce_sum | solution.py:33
  957.3 16.8 %fusion.197 = (f32[2048]{0:T(1024)S(1)}, f32[2048]{0:T(1024)S(1)}, f32[2048]{0:T(1024)S(1)}, f32[2048]{0:T(1024)S(1)}, f32[2048]{0:T(1024)S(1)}, /*index=5*/f32[2048]{0:T(1024)}) fusion(f32[2048]{0:T(1024)S(1)} %bitcast.767, f32[1024]{0:T(1024)S(1)} %bitcast.815, f32[2048]{0:T(1024)S(1)} %bitcast.764, f32[1024]{0:T(1024)S(1)} %bitcast.818, ...), kind=kLoop, calls=%fused_computation.289.clone.1 | loop fusion | flops 85970944 | bytes 122880 | tf_op jit(solution)/shard_map/while/body/eval_jaxpr/reduce_sum | solution.py:33
  975.5 40.3 %all-gather.35.cloned.1.call-done = f32[128,6,4096]{2,1,0:T(8,128)} async-done(((f32[1,6,4096]{2,1,0:T(8,128)}), f32[128,6,4096]{2,1,0:T(8,128)}) %all-gather.35.cloned.1.call-update) | async-done | bytes 12582928 | tf_op jit(solution)/shard_map/all_gather | solution.py:12
  1015.8 7.6 reduce_sum.529
  1024.1 32.9 %while.87 = (s32[]{:T(128)}, f32[2,6,2048]{2,1,0:T(8,128)S(1)}, f32[3,1024]{1,0:T(4,128)S(1)}, f32[2,6,2048]{2,1,0:T(8,128)S(1)}, f32[3,1024]{1,0:T(4,128)S(1)},...) while((s32[]{:T(128)}, f32[2,6,2048]{2,1,0:T(8,128)S(1)}, ...), condition=%wide.region_78.79_spmd, body=%wide.region_71.78_spmd.sunk | while | flops 85970952 | bytes 499925 | solution.py:42
  1024.2 16.2 %fusion.199 = (f32[2048]{0:T(1024)S(1)}, f32[2048]{0:T(1024)S(1)}, f32[2048]{0:T(1024)S(1)}, f32[2048]{0:T(1024)S(1)}, f32[2048]{0:T(1024)S(1)}, /*index=5*/f32[2048]{0:T(1024)S(1)}) fusion(f32[2048]{0:T(1024)S(1)} %bitcast.773, f32[1024]{0:T(1024)S(1)} %bitcast.821, f32[2048]{0:T(1024)S(1)} %bitcast.770, f32[1024]{0:T(1024)S(1)} %bitcast.824, ...), kind=kLoop, calls=%fused_computation.329.clone.1 | loop fusion | flops 85970944 | bytes 122880 | tf_op jit(solution)/shard_map/while/body/eval_jaxpr/reduce_sum | solution.py:33
  1040.6 16.2 %fusion.199 = (f32[2048]{0:T(1024)S(1)}, f32[2048]{0:T(1024)S(1)}, f32[2048]{0:T(1024)S(1)}, f32[2048]{0:T(1024)S(1)}, f32[2048]{0:T(1024)S(1)}, /*index=5*/f32[2048]{0:T(1024)S(1)}) fusion(f32[2048]{0:T(1024)S(1)} %bitcast.773, f32[1024]{0:T(1024)S(1)} %bitcast.821, f32[2048]{0:T(1024)S(1)} %bitcast.770, f32[1024]{0:T(1024)S(1)} %bitcast.824, ...), kind=kLoop, calls=%fused_computation.329.clone.1 | loop fusion | flops 85970944 | bytes 122880 | tf_op jit(solution)/shard_map/while/body/eval_jaxpr/reduce_sum | solution.py:33
  1057.0 46.3 %all-gather.37.cloned.1.call-done = f32[128,6,4096]{2,1,0:T(8,128)} async-done(((f32[1,6,4096]{2,1,0:T(8,128)}), f32[128,6,4096]{2,1,0:T(8,128)}) %all-gather.37.cloned.1.call-update) | async-done | bytes 12582928 | tf_op jit(solution)/shard_map/all_gather | solution.py:12
  1103.3 6.9 reduce_sum.530
  1117.6 72.7 %all-gather.39.cloned.1.call-done = f32[128,6,4096]{2,1,0:T(8,128)} async-done(((f32[1,6,4096]{2,1,0:T(8,128)}), f32[128,6,4096]{2,1,0:T(8,128)}) %all-gather.39.cloned.1.call-update) | async-done | bytes 12582928 | tf_op jit(solution)/shard_map/all_gather | solution.py:12
  1190.3 6.9 reduce_sum.531
  1197.5 1.4 scatter_fusion.5
  (224 shorter events, 41.9 us)
Async XLA Ops:
  7.2 362.1 %all-gather.25.cloned.1.call-start = ((), (), s32[]{:S(2)}) async-start(), calls=%async_computation | async-start | bytes 16908288 | tf_op jit(solution)/shard_map/all_gather | solution.py:12
  78.7 11.5 copy-start.19
  289.2 0.7 copy-start.5
  289.8 166.4 %all-gather.29.cloned.1.call-start = ((), (), s32[]{:S(2)}) async-start(), calls=%async_computation.2 | async-start | bytes 16908288 | tf_op jit(solution)/shard_map/all_gather | solution.py:12
  325.2 51.0 %copy-start.6 = (f32[2,6,2048]{2,1,0:T(8,128)}, f32[2,6,2048]{2,1,0:T(8,128)S(1)}, u32[]{:S(2)}) copy-start(f32[2,6,2048]{2,1,0:T(8,128)S(1)} %get-tuple-element.232) | copy-start | bytes 294916
  376.2 166.9 %all-gather.31.cloned.1.call-start = ((), (), s32[]{:S(2)}) async-start(), calls=%async_computation.3 | async-start | bytes 16908288 | tf_op jit(solution)/shard_map/all_gather | solution.py:12
  411.4 51.8 %copy-start.7 = (f32[2,6,2048]{2,1,0:T(8,128)}, f32[2,6,2048]{2,1,0:T(8,128)S(1)}, u32[]{:S(2)}) copy-start(f32[2,6,2048]{2,1,0:T(8,128)S(1)} %get-tuple-element.235) | copy-start | bytes 294916
  463.2 196.7 %all-gather.33.cloned.1.call-start = ((), (), s32[]{:S(2)}) async-start(), calls=%async_computation.4 | async-start | bytes 16908288 | tf_op jit(solution)/shard_map/all_gather | solution.py:12
  496.7 53.3 %copy-start.8 = (f32[2,6,2048]{2,1,0:T(8,128)}, f32[2,6,2048]{2,1,0:T(8,128)S(1)}, u32[]{:S(2)}) copy-start(f32[2,6,2048]{2,1,0:T(8,128)S(1)} %get-tuple-element.238) | copy-start | bytes 294916
  496.8 53.6 %copy-start.12 = (f32[3,1024]{1,0:T(4,128)S(1)}, f32[3,1024]{1,0:T(4,128)}, u32[]{:S(2)}) copy-start(f32[3,1024]{1,0:T(4,128)} %param.23) | copy-start | bytes 36868
  496.8 53.9 %copy-start.13 = (f32[3,1024]{1,0:T(4,128)S(1)}, f32[3,1024]{1,0:T(4,128)}, u32[]{:S(2)}) copy-start(f32[3,1024]{1,0:T(4,128)} %param.25) | copy-start | bytes 36868
  496.8 54.1 %copy-start.14 = (f32[3,1024]{1,0:T(4,128)S(1)}, f32[3,1024]{1,0:T(4,128)}, u32[]{:S(2)}) copy-start(f32[3,1024]{1,0:T(4,128)} %param.24) | copy-start | bytes 36868
  496.8 54.9 %copy-start.15 = (f32[3,1024]{1,0:T(4,128)S(1)}, f32[3,1024]{1,0:T(4,128)}, u32[]{:S(2)}) copy-start(f32[3,1024]{1,0:T(4,128)} %param.26) | copy-start | bytes 36868
  550.1 378.7 %all-gather.27.cloned.1.call-start = ((), (), s32[]{:S(2)}) async-start(), calls=%async_computation.1 | async-start | bytes 16908288 | tf_op jit(solution)/shard_map/all_gather | solution.py:12
  659.6 14.9 %copy-start.16 = (s32[1024]{0:T(1024)}, s32[1024]{0:T(1024)S(1)}, u32[]{:S(2)}) copy-start(s32[1024]{0:T(1024)S(1)} %pad_clamp_fusion) | copy-start | bytes 12292
  668.5 75.8 %copy-start.2 = (f32[3,1024]{0,1:T(8,128)}, f32[3,1024]{0,1:T(8,128)S(1)}, u32[]{:S(2)}) copy-start(f32[3,1024]{0,1:T(8,128)S(1)} %scatter_fusion) | copy-start | bytes 36868
  670.0 74.2 %copy-start = (f32[3,1024]{0,1:T(8,128)}, f32[3,1024]{0,1:T(8,128)S(1)}, u32[]{:S(2)}) copy-start(f32[3,1024]{0,1:T(8,128)S(1)} %scatter_fusion.3) | copy-start | bytes 36868
  848.3 0.6 copy-start.9
  848.9 166.8 %all-gather.35.cloned.1.call-start = ((), (), s32[]{:S(2)}) async-start(), calls=%async_computation.5 | async-start | bytes 16908288 | tf_op jit(solution)/shard_map/all_gather | solution.py:12
  886.6 0.7 copy-start.10
  935.8 167.5 %all-gather.37.cloned.1.call-start = ((), (), s32[]{:S(2)}) async-start(), calls=%async_computation.6 | async-start | bytes 16908288 | tf_op jit(solution)/shard_map/all_gather | solution.py:12
  1023.4 166.9 %all-gather.39.cloned.1.call-start = ((), (), s32[]{:S(2)}) async-start(), calls=%async_computation.7 | async-start | bytes 16908288 | tf_op jit(solution)/shard_map/all_gather | solution.py:12
  1056.9 53.3 %copy-start.11 = (f32[2,6,2048]{2,1,0:T(8,128)}, f32[2,6,2048]{2,1,0:T(8,128)S(1)}, u32[]{:S(2)}) copy-start(f32[2,6,2048]{2,1,0:T(8,128)S(1)} %get-tuple-element.248) | copy-start | bytes 294916
  1056.9 55.2 %copy-start.17 = (s32[1024]{0:T(1024)S(1)}, s32[1024]{0:T(1024)}, u32[]{:S(2)}) copy-start(s32[1024]{0:T(1024)} %copy-done.16) | copy-start | bytes 12292
  1057.0 57.3 %copy-start.1 = (f32[3,1024]{0,1:T(8,128)S(1)}, f32[3,1024]{0,1:T(8,128)}, u32[]{:S(2)}) copy-start(f32[3,1024]{0,1:T(8,128)} %copy-done) | copy-start | bytes 36868
  1057.0 58.7 %copy-start.3 = (f32[3,1024]{0,1:T(8,128)S(1)}, f32[3,1024]{0,1:T(8,128)}, u32[]{:S(2)}) copy-start(f32[3,1024]{0,1:T(8,128)} %copy-done.2) | copy-start | bytes 36868
  1057.0 60.6 %copy-start.4 = (f32[6,4096]{1,0:T(8,128)S(1)}, f32[6,4096]{1,0:T(8,128)}, u32[]{:S(2)}) copy-start(f32[6,4096]{1,0:T(8,128)} %reduce_sum.529) | copy-start | bytes 294916
  1117.6 79.9 %copy-start.18 = (s32[256,1]{0,1:T(1,128)S(1)}, s32[256,1]{0,1:T(1,128)}, u32[]{:S(2)}) copy-start(s32[256,1]{0,1:T(1,128)} %get-tuple-element.729) | copy-start | bytes 3076
Sparse Core Ops, SparseCore 0:
  290.0 79.2 all-gather.24
  376.4 79.8 all-gather.28
  463.3 79.8 all-gather.30
  550.2 79.8 all-gather.32
  849.1 79.7 all-gather.26
  935.9 79.8 all-gather.34
  1023.5 79.8 all-gather.36
  1110.4 79.8 all-gather.38
